TPU v7x, 128 devices: a whole 4x4x4 slice. The times are simulated.
128 devices in a mesh: ctx: 16 (over z, y), head: 8 (over x, core).
Axes of the slice: x: 4, y: 4, z: 4, core: 2. Of those that a mesh axis runs over, the one named last changes fastest.
Arguments:
- queries: bfloat16 [16384, 8192], P(('ctx', 'head')), may hold values from -200 to 200
- keys: bfloat16 [16384, 1024], P(('ctx', 'head')), may hold values from -6 to 6
- values: bfloat16 [16384, 1024], P(('ctx', 'head')), may hold values from -6 to 6
- doc_lengths: int32 [8], replicated, may hold values from 1 to 3073, 16384 in all
Outputs:
- attended: bfloat16 [16384, 8192], P(('ctx', 'head'))
All inputs are finite; a program needn't handle non-finite values.
Results may differ from a plain program's by a relative error of at most 0.0024.
Values may be sent and summed in bfloat16 or wider, within the bound.
No kernel may reach another device: no remote copies, remote signals or barrier semaphores. Data moves between devices by JAX's collectives and lax.ppermute only.
A program may use at most 256 MiB of HBM per device.

v0:
```python
import functools
import math

import jax
import jax.numpy as jnp
from jax import lax
from jax.experimental import pallas as pl
from jax.experimental.pallas import tpu as pltpu
from jax.sharding import PartitionSpec as P

HD = 128
REACH = 3
Q_BLOCK = 512
K_BLOCK = 2048

MASK_FILL = -1e30
EXP2_SCALE = HD ** (-0.5) * math.log2(math.e)


def shifted(block, axis, distance):
    devices = range(lax.axis_size(axis))
    route = [(i - distance, i) for i in devices if i - distance in devices]
    return lax.ppermute(block, axis, route)


def doc_first(positions, doc_starts):
    return jnp.max(
        jnp.where(positions[:, None] >= doc_starts[None, :], doc_starts[None, :], 0), axis=1
    )


def attention_kernel(
    table_ref, q_ref, k_ref, v_ref, low_ref, o_ref, top_sc, sum_sc, acc_sc, *, groups
):
    i = pl.program_id(0)
    j = pl.program_id(1)
    tq = q_ref.shape[0]
    tk = k_ref.shape[0]
    q_base = table_ref[0]
    k_base = table_ref[1]
    need_lo = table_ref[2 + 4 * i]
    need_hi = table_ref[3 + 4 * i]
    full_lo = table_ref[4 + 4 * i]
    full_hi = table_ref[5 + 4 * i]

    @pl.when(j == 0)
    def _():
        top_sc[...] = jnp.full(top_sc.shape, MASK_FILL, jnp.float32)
        sum_sc[...] = jnp.zeros(sum_sc.shape, jnp.float32)
        acc_sc[...] = jnp.zeros(acc_sc.shape, jnp.float32)

    needed = (j >= need_lo) & (j <= need_hi)
    full = (j >= full_lo) & (j <= full_hi)

    def step(masked):
        k = k_ref[...]
        v = v_ref[...]
        if masked:
            q_pos = q_base + i * tq + lax.broadcasted_iota(jnp.int32, (tq, tk), 0)
            k_pos = k_base + j * tk + lax.broadcasted_iota(jnp.int32, (tq, tk), 1)
            allowed = (k_pos <= q_pos) & (k_pos >= low_ref[...])
        for h in range(groups):
            q = q_ref[:, h * HD : (h + 1) * HD]
            raw = lax.dot_general(
                q, k, (((1,), (1,)), ((), ())), preferred_element_type=jnp.float32
            )
            if masked:
                raw = jnp.where(allowed, raw, MASK_FILL)
            top_old = top_sc[h]
            top_new = jnp.maximum(top_old, jnp.max(raw, axis=1, keepdims=True))
            weights = jnp.exp2(raw * EXP2_SCALE - top_new * EXP2_SCALE)
            rescale = jnp.exp2((top_old - top_new) * EXP2_SCALE)
            sum_sc[h] = sum_sc[h] * rescale + jnp.sum(weights, axis=1, keepdims=True)
            update = lax.dot_general(
                weights.astype(jnp.bfloat16),
                v,
                (((1,), (0,)), ((), ())),
                preferred_element_type=jnp.float32,
            )
            acc_sc[h] = acc_sc[h] * rescale + update
            top_sc[h] = top_new

    @pl.when(needed & full)
    def _():
        step(False)

    @pl.when(needed & jnp.logical_not(full))
    def _():
        step(True)

    @pl.when(j == pl.num_programs(1) - 1)
    def _():
        for h in range(groups):
            o_ref[:, h * HD : (h + 1) * HD] = (acc_sc[h] / sum_sc[h]).astype(o_ref.dtype)


def attend(q_loc, kv_all, row_low, q_base, k_base, head_first, head_count):
    tokens = q_loc.shape[0]
    q_width = head_count * HD
    column_block = head_first // head_count
    span = kv_all.shape[0]
    groups = q_width // HD
    tq = min(Q_BLOCK, tokens)
    tk = min(K_BLOCK, span)
    nq = tokens // tq
    nk = span // tk
    firsts = q_base + jnp.arange(nq, dtype=jnp.int32) * tq
    lasts = firsts + tq - 1
    low_min = row_low[::tq]
    low_max = row_low[tq - 1 :: tq]
    need_lo = jnp.maximum((low_min - k_base) // tk, 0)
    need_hi = jnp.minimum((lasts - k_base) // tk, nk - 1)
    full_lo = -((k_base - low_max) // tk)
    full_hi = (firsts + 1 - k_base) // tk - 1
    per_block = jnp.stack([need_lo, need_hi, full_lo, full_hi], axis=1).reshape(-1)
    table = jnp.concatenate(
        [jnp.stack([q_base, k_base]).astype(jnp.int32), per_block.astype(jnp.int32)]
    )

    def kv_index(col):
        def index(i, j, table_ref):
            lo = table_ref[2 + 4 * i]
            hi = table_ref[3 + 4 * i]
            return (jnp.minimum(jnp.maximum(j, lo), hi), col)

        return index

    grid_spec = pltpu.PrefetchScalarGridSpec(
        num_scalar_prefetch=1,
        grid=(nq, nk),
        in_specs=[
            pl.BlockSpec((tq, q_width), lambda i, j, t: (i, column_block)),
            pl.BlockSpec((tk, HD), kv_index(0)),
            pl.BlockSpec((tk, HD), kv_index(1)),
            pl.BlockSpec((tq, 1), lambda i, j, t: (i, 0)),
        ],
        out_specs=pl.BlockSpec((tq, q_width), lambda i, j, t: (i, 0)),
        scratch_shapes=[
            pltpu.VMEM((groups, tq, 1), jnp.float32),
            pltpu.VMEM((groups, tq, 1), jnp.float32),
            pltpu.VMEM((groups, tq, HD), jnp.float32),
        ],
    )
    return pl.pallas_call(
        functools.partial(attention_kernel, groups=groups),
        grid_spec=grid_spec,
        out_shape=jax.ShapeDtypeStruct((tokens, q_width), jnp.bfloat16),
        compiler_params=pltpu.CompilerParams(
            dimension_semantics=("arbitrary", "arbitrary")
        ),
    )(table, q_loc, kv_all, kv_all, row_low.reshape(tokens, 1))


def shards(queries, keys, values, doc_lengths):
    rows = keys.shape[0]
    heads = keys.shape[1] // HD
    kv_pairs = jnp.concatenate(
        [keys.reshape(rows, heads, HD), values.reshape(rows, heads, HD)], axis=2
    )
    kv_loc = lax.all_to_all(kv_pairs, "head", split_axis=1, concat_axis=0, tiled=True)
    kv_loc = kv_loc.reshape(kv_loc.shape[0], 2 * HD)
    q_loc = lax.all_to_all(
        queries.reshape(rows, heads, -1), "head", split_axis=1, concat_axis=0, tiled=True
    )
    q_loc = q_loc.reshape(q_loc.shape[0], -1)
    my_index = lax.axis_index("ctx")
    tokens = q_loc.shape[0]
    doc_ends = jnp.cumsum(doc_lengths)
    doc_starts = doc_ends - doc_lengths
    row_pos = my_index * tokens + jnp.arange(tokens, dtype=jnp.int32)
    row_low = doc_first(row_pos, doc_starts).astype(jnp.int32)
    pieces = [kv_loc]
    for distance in range(1, REACH + 1):
        pieces.append(shifted(kv_loc, "ctx", distance))
    kv_all = jnp.concatenate(pieces[::-1], axis=0)
    q_base = (my_index * tokens).astype(jnp.int32)
    k_base = ((my_index - REACH) * tokens).astype(jnp.int32)
    groups = q_loc.shape[1] // HD
    returned = []
    for head_first in range(0, groups, groups // 2):
        owned = attend(q_loc, kv_all, row_low, q_base, k_base, head_first, groups // 2)
        back = lax.all_to_all(
            owned.reshape(heads, rows, -1), "head", split_axis=0, concat_axis=0, tiled=True
        )
        returned.append(back)
    joined = jnp.concatenate(returned, axis=2)
    return jnp.transpose(joined, (1, 0, 2)).reshape(rows, -1)


def solution(mesh):
    return jax.shard_map(
        shards,
        mesh=mesh,
        in_specs=(
            P(("ctx", "head"), None),
            P(("ctx", "head"), None),
            P(("ctx", "head"), None),
            P(),
        ),
        out_specs=P(("ctx", "head"), None),
        check_vma=False,
    )
```

profile of v0, /device:TPU:96, one launch (start us, length us, event | category | flops | bytes accessed | tf_op | source)
XLA Modules:
  0.0 162.6 jit_solution(18344931391754997651)
XLA Ops:
  0.0 0.0 copy-start
  0.0 0.0 copy-start.2
  0.0 0.9 copy-done
  1.0 1.1 copy_bitcast_fusion.1
  2.0 0.9 pad_maximum_fusion.1
  2.9 4.3 %all-to-all-start.1 = ((bf16[128,8,256]{2,0,1:T(8,128)(2,1)}), bf16[128,8,256]{2,0,1:T(8,128)(2,1)S(1)}, u32[]{:S(2)}, u32[]{:S(2)}) async-start(bf16[128,8,256]{2,0,1:T(8,128)(2,1)} %pad_maximum_fusion.1), calls=%async_computation.1 | async-start | bytes 1048576 | tf_op jit(solution)/shard_map/all_to_all | solution.py:160
  7.2 0.0 copy-done.2
  7.2 1.6 copy.31
  8.8 8.8 %all-to-all-done.1 = bf16[128,8,256]{2,0,1:T(8,128)(2,1)S(1)} async-done(((bf16[128,8,256]{2,0,1:T(8,128)(2,1)}), bf16[128,8,256]{2,0,1:T(8,128)(2,1)S(1)}, u32[]{:S(2)}, u32[]{:S(2)}) %all-to-all-start.1) | async-done | bytes 524320 | tf_op jit(solution)/shard_map/all_to_all | solution.py:160
  17.5 0.0 copy-start.3
  17.5 3.7 %all-to-all-start = ((bf16[128,8,1024]{2,0,1:T(8,128)(2,1)}), bf16[128,8,1024]{2,0,1:T(8,128)(2,1)S(1)}, u32[]{:S(2)}, u32[]{:S(2)}) async-start(bf16[128,8,1024]{2,0,1:T(8,128)(2,1)} %bitcast.42), calls=%async_computation | async-start | bytes 4194304 | tf_op jit(solution)/shard_map/all_to_all | solution.py:162
  21.3 0.0 copy-done.3
  21.3 0.2 reduce-window.9
  21.5 0.1 select_reduce_fusion
  21.6 0.1 slice.9
  21.7 0.1 slice.8
  21.8 3.5 %collective-permute-start.2 = (bf16[1024,256]{1,0:T(8,128)(2,1)S(1)}, bf16[1024,256]{1,0:T(8,128)(2,1)S(1)}, u32[]{:S(2)}, u32[]{:S(2)}) collective-permute-start(bf16[1024,256]{1,0:T(8,128)(2,1)S(1)} %bitcast.46), channel_id=1, source_target_pairs={{0,8},{8,16},{16,24},{24,32},{32,40},{40,48},{48,56},{56,64},{64,7... | collective-permute-start | bytes 1572872 | tf_op jit(solution)/shard_map/ppermute | solution.py:23
  25.3 4.8 %collective-permute-start.1 = (bf16[1024,256]{1,0:T(8,128)(2,1)S(1)}, bf16[1024,256]{1,0:T(8,128)(2,1)}, u32[]{:S(2)}, u32[]{:S(2)}) collective-permute-start(bf16[1024,256]{1,0:T(8,128)(2,1)S(1)} %bitcast.47), channel_id=1, source_target_pairs={{0,16},{8,24},{16,32},{24,40},{32,48},{40,56},{48,64},{56,72},{64,... | collective-permute-start | bytes 1572872 | tf_op jit(solution)/shard_map/ppermute | solution.py:23
  30.1 1.9 %collective-permute-start = (bf16[1024,256]{1,0:T(8,128)(2,1)S(1)}, bf16[1024,256]{1,0:T(8,128)(2,1)}, u32[]{:S(2)}, u32[]{:S(2)}) collective-permute-start(bf16[1024,256]{1,0:T(8,128)(2,1)S(1)} %bitcast.48), channel_id=1, source_target_pairs={{0,24},{8,32},{16,40},{24,48},{32,56},{40,64},{48,72},{56,80},{64,... | collective-permute-start | bytes 1572872 | tf_op jit(solution)/shard_map/ppermute | solution.py:23
  32.1 0.1 copy.17
  32.2 0.1 reshape.186
  32.3 1.0 copy.21.low_ref
  33.3 0.6 pad_add_fusion.1.table_ref
  33.9 6.4 %collective-permute-done.2 = bf16[1024,256]{1,0:T(8,128)(2,1)S(1)} collective-permute-done((bf16[1024,256]{1,0:T(8,128)(2,1)S(1)}, bf16[1024,256]{1,0:T(8,128)(2,1)S(1)}, u32[]{:S(2)}, u32[]{:S(2)}) %collective-permute-start.2) | collective-permute-done | bytes 524320 | tf_op jit(solution)/shard_map/ppermute | solution.py:23
  40.3 16.9 %collective-permute-done.1 = bf16[1024,256]{1,0:T(8,128)(2,1)} collective-permute-done((bf16[1024,256]{1,0:T(8,128)(2,1)S(1)}, bf16[1024,256]{1,0:T(8,128)(2,1)}, u32[]{:S(2)}, u32[]{:S(2)}) %collective-permute-start.1) | collective-permute-done | bytes 524320 | tf_op jit(solution)/shard_map/ppermute | solution.py:23
  57.2 5.5 %collective-permute-done = bf16[1024,256]{1,0:T(8,128)(2,1)} collective-permute-done((bf16[1024,256]{1,0:T(8,128)(2,1)S(1)}, bf16[1024,256]{1,0:T(8,128)(2,1)}, u32[]{:S(2)}, u32[]{:S(2)}) %collective-permute-start) | collective-permute-done | bytes 524320 | tf_op jit(solution)/shard_map/ppermute | solution.py:23
  62.7 2.7 %pad_maximum_fusion.k_ref.v_ref = bf16[4096,256]{1,0:T(8,128)(2,1)} fusion(bf16[1024,256]{1,0:T(8,128)(2,1)S(1)} %bitcast.49, bf16[1024,256]{1,0:T(8,128)(2,1)S(1)} %collective-permute-done.2, bf16[1024,256]{1,0:T(8,128)(2,1)} %collective-permute-done.1, bf16[1024,256]{1,0:T(8,128)(2,1)} %collective-permute-done), kind=kLoop, calls=%fused_computation.1 | loop fusion | flops 8388608 | bytes 4194304 | tf_op jit(solution)/shard_map/concatenate | solution.py:175
  65.4 0.0 all-to-all-done
  65.4 0.0 copy-start.1
  65.4 1.3 copy-done.1
  66.7 34.4 %shard_map.47 = bf16[1024,512]{1,0:T(8,128)(2,1)} custom-call(s32[10]{0:T(128)} %pad_add_fusion.1.table_ref, bf16[1024,1024]{1,0:T(8,128)(2,1)} %bitcast.40, bf16[4096,256]{1,0:T(8,128)(2,1)} %pad_maximum_fusion.k_ref.v_ref, bf16[4096,256]{1,0:T(8,128)(2,1)} %pad_maximum_fusion.k_ref.v_ref, s32[1024,1]{1,0:T(8,128)} %copy.21.low_ref), custom_call_target="tpu_custom_call" | custom-call | tf_op jit(solution)/shard_map/pallas_call | solution.py:144
  101.1 4.5 %all-to-all-start.3 = ((bf16[8,128,512]{2,1,0:T(8,128)(2,1)}), bf16[8,128,512]{2,1,0:T(8,128)(2,1)S(1)}, u32[]{:S(2)}, u32[]{:S(2)}) async-start(bf16[8,128,512]{2,1,0:T(8,128)(2,1)} %bitcast.43), calls=%async_computation.3 | async-start | bytes 2097152 | tf_op jit(solution)/shard_map/all_to_all | solution.py:182
  105.5 34.3 %shard_map.46 = bf16[1024,512]{1,0:T(8,128)(2,1)} custom-call(s32[10]{0:T(128)} %pad_add_fusion.1.table_ref, bf16[1024,1024]{1,0:T(8,128)(2,1)} %bitcast.41, bf16[4096,256]{1,0:T(8,128)(2,1)} %pad_maximum_fusion.k_ref.v_ref, bf16[4096,256]{1,0:T(8,128)(2,1)} %pad_maximum_fusion.k_ref.v_ref, s32[1024,1]{1,0:T(8,128)} %copy.21.low_ref), custom_call_target="tpu_custom_call" | custom-call | tf_op jit(solution)/shard_map/pallas_call | solution.py:144
  139.9 0.0 all-to-all-done.3
  139.9 20.9 %all_to_all.40 = bf16[8,128,512]{2,1,0:T(8,128)(2,1)S(1)} all-to-all(bf16[8,128,512]{2,1,0:T(8,128)(2,1)} %bitcast.44), channel_id=1, replica_groups=mesh['ctx'=16,'head'=8] {'head'}, dimensions={0} | all-to-all | bytes 2097152 | tf_op jit(solution)/shard_map/all_to_all | solution.py:182
  160.8 0.3 maximum_bitcast_fusion
  161.0 1.6 copy.27
  (5 shorter events, 0.0 us)
Async XLA Ops:
  0.0 1.0 copy-start
  0.0 7.2 %copy-start.2 = (bf16[128,8192]{1,0:T(8,128)(2,1)S(1)}, bf16[128,8192]{1,0:T(8,128)(2,1)}, u32[]{:S(2)}) copy-start(bf16[128,8192]{1,0:T(8,128)(2,1)} %param.4) | copy-start | bytes 6291460
  2.9 14.6 %all-to-all-start.1 = ((bf16[128,8,256]{2,0,1:T(8,128)(2,1)}), bf16[128,8,256]{2,0,1:T(8,128)(2,1)S(1)}, u32[]{:S(2)}, u32[]{:S(2)}) async-start(bf16[128,8,256]{2,0,1:T(8,128)(2,1)} %pad_maximum_fusion.1), calls=%async_computation.1 | async-start | bytes 1048576 | tf_op jit(solution)/shard_map/all_to_all | solution.py:160
  17.5 3.8 %copy-start.3 = (s32[8]{0:T(128)S(1)}, s32[8]{0:T(128)}, u32[]{:S(2)}) copy-start(s32[8]{0:T(128)} %param.7) | copy-start | bytes 100
  17.5 47.9 %all-to-all-start = ((bf16[128,8,1024]{2,0,1:T(8,128)(2,1)}), bf16[128,8,1024]{2,0,1:T(8,128)(2,1)S(1)}, u32[]{:S(2)}, u32[]{:S(2)}) async-start(bf16[128,8,1024]{2,0,1:T(8,128)(2,1)} %bitcast.42), calls=%async_computation | async-start | bytes 4194304 | tf_op jit(solution)/shard_map/all_to_all | solution.py:162
  21.8 18.6 %collective-permute-start.2 = (bf16[1024,256]{1,0:T(8,128)(2,1)S(1)}, bf16[1024,256]{1,0:T(8,128)(2,1)S(1)}, u32[]{:S(2)}, u32[]{:S(2)}) collective-permute-start(bf16[1024,256]{1,0:T(8,128)(2,1)S(1)} %bitcast.46), channel_id=1, source_target_pairs={{0,8},{8,16},{16,24},{24,32},{32,40},{40,48},{48,56},{56,64},{64,7... | collective-permute-start | bytes 1572872 | tf_op jit(solution)/shard_map/ppermute | solution.py:23
  25.3 32.0 %collective-permute-start.1 = (bf16[1024,256]{1,0:T(8,128)(2,1)S(1)}, bf16[1024,256]{1,0:T(8,128)(2,1)}, u32[]{:S(2)}, u32[]{:S(2)}) collective-permute-start(bf16[1024,256]{1,0:T(8,128)(2,1)S(1)} %bitcast.47), channel_id=1, source_target_pairs={{0,16},{8,24},{16,32},{24,40},{32,48},{40,56},{48,64},{56,72},{64,... | collective-permute-start | bytes 1572872 | tf_op jit(solution)/shard_map/ppermute | solution.py:23
  30.1 32.6 %collective-permute-start = (bf16[1024,256]{1,0:T(8,128)(2,1)S(1)}, bf16[1024,256]{1,0:T(8,128)(2,1)}, u32[]{:S(2)}, u32[]{:S(2)}) collective-permute-start(bf16[1024,256]{1,0:T(8,128)(2,1)S(1)} %bitcast.48), channel_id=1, source_target_pairs={{0,24},{8,32},{16,40},{24,48},{32,56},{40,64},{48,72},{56,80},{64,... | collective-permute-start | bytes 1572872 | tf_op jit(solution)/shard_map/ppermute | solution.py:23
  65.4 1.3 copy-start.1
  101.1 38.8 %all-to-all-start.3 = ((bf16[8,128,512]{2,1,0:T(8,128)(2,1)}), bf16[8,128,512]{2,1,0:T(8,128)(2,1)S(1)}, u32[]{:S(2)}, u32[]{:S(2)}) async-start(bf16[8,128,512]{2,1,0:T(8,128)(2,1)} %bitcast.43), calls=%async_computation.3 | async-start | bytes 2097152 | tf_op jit(solution)/shard_map/all_to_all | solution.py:182
where the time goes:
time: 163 us
  Pallas kernels  68.7 us (42%)
  waiting for transfers between devices  37.6 us (23%)
  starting transfers between devices  22.7 us (14%)
  blocking collectives  20.9 us (13%)
  local copies, waits for them, and re-layouts  7.86 us (5%)
  other arithmetic  4.75 us (3%)
    pallas_call x2, Pallas kernels, attend(): pl.pallas_call(functools.partial(attention_kernel, groups=groups), grid_s...  68.7 us
    ppermute x3, waiting for transfers between devices, shifted(): return lax.ppermute(block, axis, route)  28.8 us
    all_to_all x1, blocking collectives, shards(): lax.all_to_all(owned.reshape(heads, rows, -1), 'head', split_axis=0, conc...  20.9 us
    ppermute x3, starting transfers between devices, shifted(): return lax.ppermute(block, axis, route)  10.2 us
    all_to_all x1, waiting for transfers between devices, shards(): lax.all_to_all(kv_pairs, 'head', split_axis=1, concat_axis=0, tiled=True)  8.78 us
    all_to_all x1, starting transfers between devices, shards(): lax.all_to_all(owned.reshape(heads, rows, -1), 'head', split_axis=0, conc...  4.46 us
    all_to_all x1, starting transfers between devices, shards(): lax.all_to_all(kv_pairs, 'head', split_axis=1, concat_axis=0, tiled=True)  4.3 us
    all_to_all x1, starting transfers between devices, shards(): lax.all_to_all(queries.reshape(rows, heads, -1), 'head', split_axis=1, co...  3.74 us
  transfers between devices with their start and end apart: 6, of which 4 were waited for; matrix products, arithmetic and copies ran while one was open for 4% of the time, Pallas kernels for 21%

commit v1 on v0

--- a/solution.py
+++ b/solution.py
@@ -12,6 +12,7 @@
 REACH = 3
 Q_BLOCK = 512
 K_BLOCK = 2048
+HEAD_SPLIT = (3, 3, 2)
 
 MASK_FILL = -1e30
 EXP2_SCALE = HD ** (-0.5) * math.log2(math.e)
@@ -177,8 +178,10 @@
     k_base = ((my_index - REACH) * tokens).astype(jnp.int32)
     groups = q_loc.shape[1] // HD
     returned = []
-    for head_first in range(0, groups, groups // 2):
-        owned = attend(q_loc, kv_all, row_low, q_base, k_base, head_first, groups // 2)
+    head_first = 0
+    for head_count in HEAD_SPLIT:
+        owned = attend(q_loc, kv_all, row_low, q_base, k_base, head_first, head_count)
+        head_first += head_count
         back = lax.all_to_all(
             owned.reshape(heads, rows, -1), "head", split_axis=0, concat_axis=0, tiled=True
         )

time: 163 us -> 172 us (1.055)
  the two profiles are of different devices: /device:TPU:96 before, /device:TPU:40 now
where the time goes in v1:
time: 172 us; the launch traced here: 169 us
  Pallas kernels  75.1 us (44%)
  waiting for transfers between devices  33.9 us (20%)
  starting transfers between devices  29.3 us (17%)
  blocking collectives  18 us (10%)
  local copies, waits for them, and re-layouts  7.84 us (5%)
  other arithmetic  4.8 us (3%)
    pallas_call x3, Pallas kernels, attend(): pl.pallas_call(functools.partial(attention_kernel, groups=groups), grid_s...  75.1 us
    ppermute x3, waiting for transfers between devices, shifted(): return lax.ppermute(block, axis, route)  25.1 us
    all_to_all x1, blocking collectives, shards(): lax.all_to_all(owned.reshape(heads, rows, -1), 'head', split_axis=0, conc...  18 us
    ppermute x3, starting transfers between devices, shifted(): return lax.ppermute(block, axis, route)  12 us
    all_to_all x2, starting transfers between devices, shards(): lax.all_to_all(owned.reshape(heads, rows, -1), 'head', split_axis=0, conc...  9.28 us
    all_to_all x1, waiting for transfers between devices, shards(): lax.all_to_all(kv_pairs, 'head', split_axis=1, concat_axis=0, tiled=True)  8.78 us
    all_to_all x1, starting transfers between devices, shards(): lax.all_to_all(kv_pairs, 'head', split_axis=1, concat_axis=0, tiled=True)  4.3 us
    all_to_all x1, starting transfers between devices, shards(): lax.all_to_all(queries.reshape(rows, heads, -1), 'head', split_axis=1, co...  3.74 us
  transfers between devices with their start and end apart: 7, of which 4 were waited for; matrix products, arithmetic and copies ran while one was open for 4% of the time, Pallas kernels for 32%

profile of v1, /device:TPU:40, one launch (start us, length us, event | category | flops | bytes accessed | tf_op | source)
XLA Modules:
  0.0 169.1 jit_solution(3193667171267036822)
XLA Ops:
  0.0 0.0 copy-start
  0.0 0.0 copy-start.2
  0.0 0.9 copy-done
  1.0 1.1 copy_bitcast_fusion.1
  2.0 0.9 pad_maximum_fusion.1
  2.9 4.3 %all-to-all-start.1 = ((bf16[128,8,256]{2,0,1:T(8,128)(2,1)}), bf16[128,8,256]{2,0,1:T(8,128)(2,1)S(1)}, u32[]{:S(2)}, u32[]{:S(2)}) async-start(bf16[128,8,256]{2,0,1:T(8,128)(2,1)} %pad_maximum_fusion.1), calls=%async_computation.1 | async-start | bytes 1048576 | tf_op jit(solution)/shard_map/all_to_all | solution.py:161
  7.2 0.0 copy-done.2
  7.2 1.6 copy.33
  8.8 8.8 %all-to-all-done.1 = bf16[128,8,256]{2,0,1:T(8,128)(2,1)S(1)} async-done(((bf16[128,8,256]{2,0,1:T(8,128)(2,1)}), bf16[128,8,256]{2,0,1:T(8,128)(2,1)S(1)}, u32[]{:S(2)}, u32[]{:S(2)}) %all-to-all-start.1) | async-done | bytes 524320 | tf_op jit(solution)/shard_map/all_to_all | solution.py:161
  17.5 0.0 copy-start.3
  17.6 3.7 %all-to-all-start = ((bf16[128,8,1024]{2,0,1:T(8,128)(2,1)}), bf16[128,8,1024]{2,0,1:T(8,128)(2,1)S(1)}, u32[]{:S(2)}, u32[]{:S(2)}) async-start(bf16[128,8,1024]{2,0,1:T(8,128)(2,1)} %bitcast.44), calls=%async_computation | async-start | bytes 4194304 | tf_op jit(solution)/shard_map/all_to_all | solution.py:163
  21.3 0.0 copy-done.3
  21.3 0.2 reduce-window.9
  21.5 0.1 select_reduce_fusion
  21.6 0.1 slice.5
  21.7 0.1 slice.4
  21.8 3.5 %collective-permute-start.2 = (bf16[1024,256]{1,0:T(8,128)(2,1)S(1)}, bf16[1024,256]{1,0:T(8,128)(2,1)S(1)}, u32[]{:S(2)}, u32[]{:S(2)}) collective-permute-start(bf16[1024,256]{1,0:T(8,128)(2,1)S(1)} %bitcast.48), channel_id=1, source_target_pairs={{0,8},{8,16},{16,24},{24,32},{32,40},{40,48},{48,56},{56,64},{64,7... | collective-permute-start | bytes 1572872 | tf_op jit(solution)/shard_map/ppermute | solution.py:24
  25.3 4.2 %collective-permute-start.1 = (bf16[1024,256]{1,0:T(8,128)(2,1)S(1)}, bf16[1024,256]{1,0:T(8,128)(2,1)}, u32[]{:S(2)}, u32[]{:S(2)}) collective-permute-start(bf16[1024,256]{1,0:T(8,128)(2,1)S(1)} %bitcast.49), channel_id=1, source_target_pairs={{0,16},{8,24},{16,32},{24,40},{32,48},{40,56},{48,64},{56,72},{64,... | collective-permute-start | bytes 1572872 | tf_op jit(solution)/shard_map/ppermute | solution.py:24
  29.5 4.3 %collective-permute-start = (bf16[1024,256]{1,0:T(8,128)(2,1)S(1)}, bf16[1024,256]{1,0:T(8,128)(2,1)}, u32[]{:S(2)}, u32[]{:S(2)}) collective-permute-start(bf16[1024,256]{1,0:T(8,128)(2,1)S(1)} %bitcast.50), channel_id=1, source_target_pairs={{0,24},{8,32},{16,40},{24,48},{32,56},{40,64},{48,72},{56,80},{64,... | collective-permute-start | bytes 1572872 | tf_op jit(solution)/shard_map/ppermute | solution.py:24
  33.9 0.1 copy.18
  34.0 0.1 reshape.191
  34.1 1.0 copy.22.low_ref
  35.1 0.7 pad_add_fusion.1.table_ref
  35.7 2.7 %collective-permute-done.2 = bf16[1024,256]{1,0:T(8,128)(2,1)S(1)} collective-permute-done((bf16[1024,256]{1,0:T(8,128)(2,1)S(1)}, bf16[1024,256]{1,0:T(8,128)(2,1)S(1)}, u32[]{:S(2)}, u32[]{:S(2)}) %collective-permute-start.2) | collective-permute-done | bytes 524320 | tf_op jit(solution)/shard_map/ppermute | solution.py:24
  38.4 6.1 %collective-permute-done.1 = bf16[1024,256]{1,0:T(8,128)(2,1)} collective-permute-done((bf16[1024,256]{1,0:T(8,128)(2,1)S(1)}, bf16[1024,256]{1,0:T(8,128)(2,1)}, u32[]{:S(2)}, u32[]{:S(2)}) %collective-permute-start.1) | collective-permute-done | bytes 524320 | tf_op jit(solution)/shard_map/ppermute | solution.py:24
  44.5 16.3 %collective-permute-done = bf16[1024,256]{1,0:T(8,128)(2,1)} collective-permute-done((bf16[1024,256]{1,0:T(8,128)(2,1)S(1)}, bf16[1024,256]{1,0:T(8,128)(2,1)}, u32[]{:S(2)}, u32[]{:S(2)}) %collective-permute-start) | collective-permute-done | bytes 524320 | tf_op jit(solution)/shard_map/ppermute | solution.py:24
  60.8 2.7 %pad_maximum_fusion.k_ref.v_ref = bf16[4096,256]{1,0:T(8,128)(2,1)} fusion(bf16[1024,256]{1,0:T(8,128)(2,1)S(1)} %bitcast.51, bf16[1024,256]{1,0:T(8,128)(2,1)S(1)} %collective-permute-done.2, bf16[1024,256]{1,0:T(8,128)(2,1)} %collective-permute-done.1, bf16[1024,256]{1,0:T(8,128)(2,1)} %collective-permute-done), kind=kLoop, calls=%fused_computation.1 | loop fusion | flops 8388608 | bytes 4194304 | tf_op jit(solution)/shard_map/concatenate | solution.py:176
  63.5 0.0 all-to-all-done
  63.5 0.0 copy-start.1
  63.5 1.3 copy-done.1
  64.8 20.5 %shard_map.48 = bf16[1024,256]{1,0:T(8,128)(2,1)} custom-call(s32[10]{0:T(128)} %pad_add_fusion.1.table_ref, bf16[1024,1024]{1,0:T(8,128)(2,1)} %bitcast.41, bf16[4096,256]{1,0:T(8,128)(2,1)} %pad_maximum_fusion.k_ref.v_ref, bf16[4096,256]{1,0:T(8,128)(2,1)} %pad_maximum_fusion.k_ref.v_ref, s32[1024,1]{1,0:T(8,128)} %copy.22.low_ref), custom_call_target="tpu_custom_call" | custom-call | tf_op jit(solution)/shard_map/pallas_call | solution.py:145
  85.3 4.5 %all-to-all-start.4 = ((bf16[8,128,256]{2,1,0:T(8,128)(2,1)}), bf16[8,128,256]{2,1,0:T(8,128)(2,1)S(1)}, u32[]{:S(2)}, u32[]{:S(2)}) async-start(bf16[8,128,256]{2,1,0:T(8,128)(2,1)} %bitcast.52), calls=%async_computation.4 | async-start | bytes 1048576 | tf_op jit(solution)/shard_map/all_to_all | solution.py:185
  89.8 27.3 %shard_map.47 = bf16[1024,384]{1,0:T(8,128)(2,1)} custom-call(s32[10]{0:T(128)} %pad_add_fusion.1.table_ref, bf16[1024,1024]{1,0:T(8,128)(2,1)} %bitcast.42, bf16[4096,256]{1,0:T(8,128)(2,1)} %pad_maximum_fusion.k_ref.v_ref, bf16[4096,256]{1,0:T(8,128)(2,1)} %pad_maximum_fusion.k_ref.v_ref, s32[1024,1]{1,0:T(8,128)} %copy.22.low_ref), custom_call_target="tpu_custom_call" | custom-call | tf_op jit(solution)/shard_map/pallas_call | solution.py:145
  117.1 0.0 all-to-all-done.4
  117.1 4.8 %all-to-all-start.3 = ((bf16[8,128,384]{2,1,0:T(8,128)(2,1)}), bf16[8,128,384]{2,1,0:T(8,128)(2,1)S(1)}, u32[]{:S(2)}, u32[]{:S(2)}) async-start(bf16[8,128,384]{2,1,0:T(8,128)(2,1)} %bitcast.45), calls=%async_computation.3 | async-start | bytes 1572864 | tf_op jit(solution)/shard_map/all_to_all | solution.py:185
  121.9 27.3 %shard_map.46 = bf16[1024,384]{1,0:T(8,128)(2,1)} custom-call(s32[10]{0:T(128)} %pad_add_fusion.1.table_ref, bf16[1024,1024]{1,0:T(8,128)(2,1)} %bitcast.43, bf16[4096,256]{1,0:T(8,128)(2,1)} %pad_maximum_fusion.k_ref.v_ref, bf16[4096,256]{1,0:T(8,128)(2,1)} %pad_maximum_fusion.k_ref.v_ref, s32[1024,1]{1,0:T(8,128)} %copy.22.low_ref), custom_call_target="tpu_custom_call" | custom-call | tf_op jit(solution)/shard_map/pallas_call | solution.py:145
  149.2 0.0 all-to-all-done.3
  149.2 18.0 %all_to_all.45 = bf16[8,128,384]{2,1,0:T(8,128)(2,1)S(1)} all-to-all(bf16[8,128,384]{2,1,0:T(8,128)(2,1)} %bitcast.46), channel_id=1, replica_groups=mesh['ctx'=16,'head'=8] {'head'}, dimensions={0} | all-to-all | bytes 1572864 | tf_op jit(solution)/shard_map/all_to_all | solution.py:185
  167.2 0.3 maximum_bitcast_fusion
  167.5 1.6 copy.29
  (5 shorter events, 0.0 us)
Async XLA Ops:
  0.0 1.0 copy-start
  0.0 7.2 %copy-start.2 = (bf16[128,8192]{1,0:T(8,128)(2,1)S(1)}, bf16[128,8192]{1,0:T(8,128)(2,1)}, u32[]{:S(2)}) copy-start(bf16[128,8192]{1,0:T(8,128)(2,1)} %param.4) | copy-start | bytes 6291460
  2.9 14.6 %all-to-all-start.1 = ((bf16[128,8,256]{2,0,1:T(8,128)(2,1)}), bf16[128,8,256]{2,0,1:T(8,128)(2,1)S(1)}, u32[]{:S(2)}, u32[]{:S(2)}) async-start(bf16[128,8,256]{2,0,1:T(8,128)(2,1)} %pad_maximum_fusion.1), calls=%async_computation.1 | async-start | bytes 1048576 | tf_op jit(solution)/shard_map/all_to_all | solution.py:161
  17.5 3.8 %copy-start.3 = (s32[8]{0:T(128)S(1)}, s32[8]{0:T(128)}, u32[]{:S(2)}) copy-start(s32[8]{0:T(128)} %param.7) | copy-start | bytes 100
  17.6 45.9 %all-to-all-start = ((bf16[128,8,1024]{2,0,1:T(8,128)(2,1)}), bf16[128,8,1024]{2,0,1:T(8,128)(2,1)S(1)}, u32[]{:S(2)}, u32[]{:S(2)}) async-start(bf16[128,8,1024]{2,0,1:T(8,128)(2,1)} %bitcast.44), calls=%async_computation | async-start | bytes 4194304 | tf_op jit(solution)/shard_map/all_to_all | solution.py:163
  21.8 16.6 %collective-permute-start.2 = (bf16[1024,256]{1,0:T(8,128)(2,1)S(1)}, bf16[1024,256]{1,0:T(8,128)(2,1)S(1)}, u32[]{:S(2)}, u32[]{:S(2)}) collective-permute-start(bf16[1024,256]{1,0:T(8,128)(2,1)S(1)} %bitcast.48), channel_id=1, source_target_pairs={{0,8},{8,16},{16,24},{24,32},{32,40},{40,48},{48,56},{56,64},{64,7... | collective-permute-start | bytes 1572872 | tf_op jit(solution)/shard_map/ppermute | solution.py:24
  25.3 19.2 %collective-permute-start.1 = (bf16[1024,256]{1,0:T(8,128)(2,1)S(1)}, bf16[1024,256]{1,0:T(8,128)(2,1)}, u32[]{:S(2)}, u32[]{:S(2)}) collective-permute-start(bf16[1024,256]{1,0:T(8,128)(2,1)S(1)} %bitcast.49), channel_id=1, source_target_pairs={{0,16},{8,24},{16,32},{24,40},{32,48},{40,56},{48,64},{56,72},{64,... | collective-permute-start | bytes 1572872 | tf_op jit(solution)/shard_map/ppermute | solution.py:24
  29.5 31.3 %collective-permute-start = (bf16[1024,256]{1,0:T(8,128)(2,1)S(1)}, bf16[1024,256]{1,0:T(8,128)(2,1)}, u32[]{:S(2)}, u32[]{:S(2)}) collective-permute-start(bf16[1024,256]{1,0:T(8,128)(2,1)S(1)} %bitcast.50), channel_id=1, source_target_pairs={{0,24},{8,32},{16,40},{24,48},{32,56},{40,64},{48,72},{56,80},{64,... | collective-permute-start | bytes 1572872 | tf_op jit(solution)/shard_map/ppermute | solution.py:24
  63.5 1.3 copy-start.1
  85.3 31.8 %all-to-all-start.4 = ((bf16[8,128,256]{2,1,0:T(8,128)(2,1)}), bf16[8,128,256]{2,1,0:T(8,128)(2,1)S(1)}, u32[]{:S(2)}, u32[]{:S(2)}) async-start(bf16[8,128,256]{2,1,0:T(8,128)(2,1)} %bitcast.52), calls=%async_computation.4 | async-start | bytes 1048576 | tf_op jit(solution)/shard_map/all_to_all | solution.py:185
  117.1 32.1 %all-to-all-start.3 = ((bf16[8,128,384]{2,1,0:T(8,128)(2,1)}), bf16[8,128,384]{2,1,0:T(8,128)(2,1)S(1)}, u32[]{:S(2)}, u32[]{:S(2)}) async-start(bf16[8,128,384]{2,1,0:T(8,128)(2,1)} %bitcast.45), calls=%async_computation.3 | async-start | bytes 1572864 | tf_op jit(solution)/shard_map/all_to_all | solution.py:185

commit v2 on v0

--- a/solution.py
+++ b/solution.py
@@ -157,12 +157,16 @@
     kv_pairs = jnp.concatenate(
         [keys.reshape(rows, heads, HD), values.reshape(rows, heads, HD)], axis=2
     )
-    kv_loc = lax.all_to_all(kv_pairs, "head", split_axis=1, concat_axis=0, tiled=True)
-    kv_loc = kv_loc.reshape(kv_loc.shape[0], 2 * HD)
-    q_loc = lax.all_to_all(
-        queries.reshape(rows, heads, -1), "head", split_axis=1, concat_axis=0, tiled=True
-    )
-    q_loc = q_loc.reshape(q_loc.shape[0], -1)
+    q_width = queries.shape[1] // heads
+    both = lax.all_to_all(
+        jnp.concatenate([queries.reshape(rows, heads, q_width), kv_pairs], axis=2),
+        "head",
+        split_axis=1,
+        concat_axis=0,
+        tiled=True,
+    )
+    q_loc = both.reshape(both.shape[0], -1)
+    kv_loc = q_loc[:, q_width:]
     my_index = lax.axis_index("ctx")
     tokens = q_loc.shape[0]
     doc_ends = jnp.cumsum(doc_lengths)
@@ -175,7 +179,7 @@
     kv_all = jnp.concatenate(pieces[::-1], axis=0)
     q_base = (my_index * tokens).astype(jnp.int32)
     k_base = ((my_index - REACH) * tokens).astype(jnp.int32)
-    groups = q_loc.shape[1] // HD
+    groups = q_width // HD
     returned = []
     for head_first in range(0, groups, groups // 2):
         owned = attend(q_loc, kv_all, row_low, q_base, k_base, head_first, groups // 2)

time: 163 us -> 179 us (1.098)
  waiting for transfers between devices: 37.6 us -> 60.2 us
  starting transfers between devices: 22.7 us -> 18.2 us
  local copies, waits for them, and re-layouts: 7.86 us -> 4.93 us
    all_to_all x2 -> x1, waiting for transfers between devices: 8.79 us -> 32.4 us  [shards(): lax.all_to_all(jnp.concatenate([queries.reshape(rows, heads, q_width), kv...]
    all_to_all x2 -> x1, starting transfers between devices: 8.04 us -> 4.43 us  [shards(): lax.all_to_all(jnp.concatenate([queries.reshape(rows, heads, q_width), kv...]
    unnamed x8, local copies, waits for them, and re-layouts: 2.27 us -> 0.02 us
  transfers between devices with their start and end apart: 6 -> 5, of which waited for: 4 -> 4; matrix products, arithmetic and copies ran while one was open for 4% -> 1% of each run, Pallas kernels for 21% -> 19%
where the time goes in v2:
time: 179 us
  Pallas kernels  68.7 us (38%)
  waiting for transfers between devices  60.2 us (34%)
  blocking collectives  20.8 us (12%)
  starting transfers between devices  18.2 us (10%)
  other arithmetic  5.85 us (3%)
  local copies, waits for them, and re-layouts  4.93 us (3%)
    pallas_call x2, Pallas kernels, attend(): pl.pallas_call(functools.partial(attention_kernel, groups=groups), grid_s...  68.7 us
    all_to_all x1, waiting for transfers between devices, shards(): lax.all_to_all(jnp.concatenate([queries.reshape(rows, heads, q_width), kv...  32.4 us
    ppermute x3, waiting for transfers between devices, shifted(): return lax.ppermute(block, axis, route)  27.9 us
    all_to_all x1, blocking collectives, shards(): lax.all_to_all(owned.reshape(heads, rows, -1), 'head', split_axis=0, conc...  20.8 us
    ppermute x3, starting transfers between devices, shifted(): return lax.ppermute(block, axis, route)  10.2 us
    all_to_all x1, starting transfers between devices, shards(): lax.all_to_all(jnp.concatenate([queries.reshape(rows, heads, q_width), kv...  4.43 us
  transfers between devices with their start and end apart: 5, of which 4 were waited for; matrix products, arithmetic and copies ran while one was open for 1% of the time, Pallas kernels for 19%

profile of v2, /device:TPU:96, one launch (start us, length us, event | category | flops | bytes accessed | tf_op | source)
XLA Modules:
  0.0 178.8 jit_solution(8578655103819998121)
XLA Ops:
  0.0 0.0 copy-start
  0.0 0.0 copy-start.2
  0.0 1.9 %copy.31 = bf16[16,8,8,1024]{3,2,0,1:T(8,128)(2,1)S(1)} copy(bf16[16,8,8,1024]{3,2,1,0:T(8,128)(2,1)} %bitcast.41) | data formatting | bytes 4194304 | tf_op jit(solution)/shard_map/reshape | solution.py:162
  1.9 0.0 copy-done
  1.9 0.0 copy-done.2
  1.9 0.1 copy_bitcast_fusion.1
  2.0 1.8 %pad_maximum_fusion = bf16[128,8,1280]{2,0,1:T(8,128)(2,1)} fusion(bf16[128,8,128]{2,0,1:T(8,128)(2,1)S(1)} %get-tuple-element.9, bf16[128,8,128]{2,0,1:T(8,128)(2,1)S(1)} %get-tuple-element.10, bf16[128,8,1024]{2,0,1:T(8,128)(2,1)S(1)} %bitcast.38), kind=kLoop, calls=%fused_computation | loop fusion | flops 7864320 | bytes 5242880 | tf_op jit(solution)/shard_map/concatenate | solution.py:162
  3.8 0.0 copy-start.3
  3.8 4.4 %all-to-all-start = ((bf16[128,8,1280]{2,0,1:T(8,128)(2,1)}), bf16[128,8,1280]{2,0,1:T(8,128)(2,1)S(1)}, u32[]{:S(2)}, u32[]{:S(2)}) async-start(bf16[128,8,1280]{2,0,1:T(8,128)(2,1)} %pad_maximum_fusion), calls=%async_computation | async-start | bytes 5242880 | tf_op jit(solution)/shard_map/all_to_all | solution.py:161
  8.2 0.0 copy-done.3
  8.2 0.2 reduce-window.9
  8.4 0.1 select_reduce_fusion
  8.5 0.1 slice.12
  8.6 0.1 slice.11
  8.7 32.4 %all-to-all-done = bf16[128,8,1280]{2,0,1:T(8,128)(2,1)S(1)} async-done(((bf16[128,8,1280]{2,0,1:T(8,128)(2,1)}), bf16[128,8,1280]{2,0,1:T(8,128)(2,1)S(1)}, u32[]{:S(2)}, u32[]{:S(2)}) %all-to-all-start) | async-done | bytes 2621472 | tf_op jit(solution)/shard_map/all_to_all | solution.py:161
  41.1 0.0 copy-start.1
  41.1 3.5 %collective-permute-start.2 = (bf16[1024,256]{1,0:T(8,128)(2,1)S(1)}, bf16[1024,256]{1,0:T(8,128)(2,1)}, u32[]{:S(2)}, u32[]{:S(2)}) collective-permute-start(bf16[1024,256]{1,0:T(8,128)(2,1)S(1)} %slice.14), channel_id=1, source_target_pairs={{0,8},{8,16},{16,24},{24,32},{32,40},{40,48},{48,56},{56,64},{64,7... | collective-permute-start | bytes 1572872 | tf_op jit(solution)/shard_map/ppermute | solution.py:23
  44.6 4.8 %collective-permute-start.1 = (bf16[1024,256]{1,0:T(8,128)(2,1)S(1)}, bf16[1024,256]{1,0:T(8,128)(2,1)}, u32[]{:S(2)}, u32[]{:S(2)}) collective-permute-start(bf16[1024,256]{1,0:T(8,128)(2,1)S(1)} %slice.14), channel_id=1, source_target_pairs={{0,16},{8,24},{16,32},{24,40},{32,48},{40,56},{48,64},{56,72},{64,... | collective-permute-start | bytes 1572872 | tf_op jit(solution)/shard_map/ppermute | solution.py:23
  49.4 1.9 %collective-permute-start = (bf16[1024,256]{1,0:T(8,128)(2,1)S(1)}, bf16[1024,256]{1,0:T(8,128)(2,1)}, u32[]{:S(2)}, u32[]{:S(2)}) collective-permute-start(bf16[1024,256]{1,0:T(8,128)(2,1)S(1)} %slice.14), channel_id=1, source_target_pairs={{0,24},{8,32},{16,40},{24,48},{32,56},{40,64},{48,72},{56,80},{64,... | collective-permute-start | bytes 1572872 | tf_op jit(solution)/shard_map/ppermute | solution.py:23
  51.4 0.1 copy.17
  51.5 0.1 reshape.182
  51.6 1.0 copy.21.low_ref
  52.6 0.7 pad_add_fusion.1.table_ref
  53.3 6.8 %collective-permute-done.2 = bf16[1024,256]{1,0:T(8,128)(2,1)} collective-permute-done((bf16[1024,256]{1,0:T(8,128)(2,1)S(1)}, bf16[1024,256]{1,0:T(8,128)(2,1)}, u32[]{:S(2)}, u32[]{:S(2)}) %collective-permute-start.2) | collective-permute-done | bytes 524320 | tf_op jit(solution)/shard_map/ppermute | solution.py:23
  60.0 16.0 %collective-permute-done.1 = bf16[1024,256]{1,0:T(8,128)(2,1)} collective-permute-done((bf16[1024,256]{1,0:T(8,128)(2,1)S(1)}, bf16[1024,256]{1,0:T(8,128)(2,1)}, u32[]{:S(2)}, u32[]{:S(2)}) %collective-permute-start.1) | collective-permute-done | bytes 524320 | tf_op jit(solution)/shard_map/ppermute | solution.py:23
  76.0 5.2 %collective-permute-done = bf16[1024,256]{1,0:T(8,128)(2,1)} collective-permute-done((bf16[1024,256]{1,0:T(8,128)(2,1)S(1)}, bf16[1024,256]{1,0:T(8,128)(2,1)}, u32[]{:S(2)}, u32[]{:S(2)}) %collective-permute-start) | collective-permute-done | bytes 524320 | tf_op jit(solution)/shard_map/ppermute | solution.py:23
  81.1 2.8 %pad_maximum_fusion.1.k_ref.v_ref = bf16[4096,256]{1,0:T(8,128)(2,1)} fusion(bf16[1024,256]{1,0:T(8,128)(2,1)S(1)} %slice.14, bf16[1024,256]{1,0:T(8,128)(2,1)} %collective-permute-done.2, bf16[1024,256]{1,0:T(8,128)(2,1)} %collective-permute-done.1, bf16[1024,256]{1,0:T(8,128)(2,1)} %collective-permute-done), kind=kLoop, calls=%fused_computation.2 | loop fusion | flops 8388608 | bytes 4194304 | tf_op jit(solution)/shard_map/concatenate | solution.py:179
  84.0 0.0 copy-done.1
  84.0 34.3 %shard_map.47 = bf16[1024,512]{1,0:T(8,128)(2,1)} custom-call(s32[10]{0:T(128)} %pad_add_fusion.1.table_ref, bf16[1024,1280]{1,0:T(8,128)(2,1)} %bitcast.36, bf16[4096,256]{1,0:T(8,128)(2,1)} %pad_maximum_fusion.1.k_ref.v_ref, bf16[4096,256]{1,0:T(8,128)(2,1)} %pad_maximum_fusion.1.k_ref.v_ref, s32[1024,1]{1,0:T(8,128)} %copy.21.low_ref), custom_call_target="tpu_custom_call" | custom-call | tf_op jit(solution)/shard_map/pallas_call | solution.py:144
  118.3 3.6 %all-to-all-start.2 = ((bf16[8,128,512]{2,1,0:T(8,128)(2,1)}), bf16[8,128,512]{2,1,0:T(8,128)(2,1)S(1)}, u32[]{:S(2)}, u32[]{:S(2)}) async-start(bf16[8,128,512]{2,1,0:T(8,128)(2,1)} %bitcast.39), calls=%async_computation.2 | async-start | bytes 2097152 | tf_op jit(solution)/shard_map/all_to_all | solution.py:186
  121.8 34.3 %shard_map.46 = bf16[1024,512]{1,0:T(8,128)(2,1)} custom-call(s32[10]{0:T(128)} %pad_add_fusion.1.table_ref, bf16[1024,1280]{1,0:T(8,128)(2,1)} %bitcast.37, bf16[4096,256]{1,0:T(8,128)(2,1)} %pad_maximum_fusion.1.k_ref.v_ref, bf16[4096,256]{1,0:T(8,128)(2,1)} %pad_maximum_fusion.1.k_ref.v_ref, s32[1024,1]{1,0:T(8,128)} %copy.21.low_ref), custom_call_target="tpu_custom_call" | custom-call | tf_op jit(solution)/shard_map/pallas_call | solution.py:144
  156.2 0.0 all-to-all-done.2
  156.2 20.8 %all_to_all.25 = bf16[8,128,512]{2,1,0:T(8,128)(2,1)S(1)} all-to-all(bf16[8,128,512]{2,1,0:T(8,128)(2,1)} %bitcast.40), channel_id=1, replica_groups=mesh['ctx'=16,'head'=8] {'head'}, dimensions={0} | all-to-all | bytes 2097152 | tf_op jit(solution)/shard_map/all_to_all | solution.py:186
  177.0 0.3 maximum_bitcast_fusion
  177.3 1.5 copy.27
  (6 shorter events, 0.1 us)
Async XLA Ops:
  0.0 1.9 %copy-start = (bf16[128,1024]{1,0:T(8,128)(2,1)S(1)}, bf16[128,1024]{1,0:T(8,128)(2,1)}, u32[]{:S(2)}) copy-start(bf16[128,1024]{1,0:T(8,128)(2,1)} %param.5) | copy-start | bytes 786436
  0.0 1.9 %copy-start.2 = (bf16[128,1024]{1,0:T(8,128)(2,1)S(1)}, bf16[128,1024]{1,0:T(8,128)(2,1)}, u32[]{:S(2)}) copy-start(bf16[128,1024]{1,0:T(8,128)(2,1)} %param.6) | copy-start | bytes 786436
  3.8 4.4 %copy-start.3 = (s32[8]{0:T(128)S(1)}, s32[8]{0:T(128)}, u32[]{:S(2)}) copy-start(s32[8]{0:T(128)} %param.7) | copy-start | bytes 100
  3.8 37.3 %all-to-all-start = ((bf16[128,8,1280]{2,0,1:T(8,128)(2,1)}), bf16[128,8,1280]{2,0,1:T(8,128)(2,1)S(1)}, u32[]{:S(2)}, u32[]{:S(2)}) async-start(bf16[128,8,1280]{2,0,1:T(8,128)(2,1)} %pad_maximum_fusion), calls=%async_computation | async-start | bytes 5242880 | tf_op jit(solution)/shard_map/all_to_all | solution.py:161
  41.1 42.9 %copy-start.1 = (bf16[128,8,1280]{2,0,1:T(8,128)(2,1)}, bf16[128,8,1280]{2,0,1:T(8,128)(2,1)S(1)}, u32[]{:S(2)}) copy-start(bf16[128,8,1280]{2,0,1:T(8,128)(2,1)S(1)} %all-to-all-done) | copy-start | bytes 7864324
  41.1 18.9 %collective-permute-start.2 = (bf16[1024,256]{1,0:T(8,128)(2,1)S(1)}, bf16[1024,256]{1,0:T(8,128)(2,1)}, u32[]{:S(2)}, u32[]{:S(2)}) collective-permute-start(bf16[1024,256]{1,0:T(8,128)(2,1)S(1)} %slice.14), channel_id=1, source_target_pairs={{0,8},{8,16},{16,24},{24,32},{32,40},{40,48},{48,56},{56,64},{64,7... | collective-permute-start | bytes 1572872 | tf_op jit(solution)/shard_map/ppermute | solution.py:23
  44.6 31.4 %collective-permute-start.1 = (bf16[1024,256]{1,0:T(8,128)(2,1)S(1)}, bf16[1024,256]{1,0:T(8,128)(2,1)}, u32[]{:S(2)}, u32[]{:S(2)}) collective-permute-start(bf16[1024,256]{1,0:T(8,128)(2,1)S(1)} %slice.14), channel_id=1, source_target_pairs={{0,16},{8,24},{16,32},{24,40},{32,48},{40,56},{48,64},{56,72},{64,... | collective-permute-start | bytes 1572872 | tf_op jit(solution)/shard_map/ppermute | solution.py:23
  49.4 31.7 %collective-permute-start = (bf16[1024,256]{1,0:T(8,128)(2,1)S(1)}, bf16[1024,256]{1,0:T(8,128)(2,1)}, u32[]{:S(2)}, u32[]{:S(2)}) collective-permute-start(bf16[1024,256]{1,0:T(8,128)(2,1)S(1)} %slice.14), channel_id=1, source_target_pairs={{0,24},{8,32},{16,40},{24,48},{32,56},{40,64},{48,72},{56,80},{64,... | collective-permute-start | bytes 1572872 | tf_op jit(solution)/shard_map/ppermute | solution.py:23
  118.3 37.9 %all-to-all-start.2 = ((bf16[8,128,512]{2,1,0:T(8,128)(2,1)}), bf16[8,128,512]{2,1,0:T(8,128)(2,1)S(1)}, u32[]{:S(2)}, u32[]{:S(2)}) async-start(bf16[8,128,512]{2,1,0:T(8,128)(2,1)} %bitcast.39), calls=%async_computation.2 | async-start | bytes 2097152 | tf_op jit(solution)/shard_map/all_to_all | solution.py:186
